TPU v7x, 256 devices: a whole 4x4x8 slice. The times are simulated.
256 devices in a mesh: exp: 64 (over y, z, core), grp: 4 (over x).
Axes of the slice: x: 4, y: 4, z: 8, core: 2. Of those that a mesh axis runs over, the one named last changes fastest.
Arguments:
- tiles: bfloat16 [1024, 256, 256], P(('exp', 'grp')), may hold values from -6 to 6
- tile_exposure: int32 [1024], P(('exp', 'grp')), may hold values from 0 to 511, as said below
- tile_patch: int32 [1024, 4], P(('exp', 'grp')), may hold values from 0 to 63, all different within a row; in each aligned block of 4 rows (0 to 3, 4 to 7, ...) at most 2 rows name the same one
- tile_offset: int32 [1024, 4, 2], P(('exp', 'grp')), may hold values from 0 to 256
- coeffs: bfloat16 [512, 10], P(('exp', 'grp')), may hold values from -2 to 2
- inv_var: bfloat16 [512], P(('exp', 'grp')), may hold values from 0.25 to 4
- vert_taps: bfloat16 [10, 41], replicated, may hold values from -1 to 1
- horiz_taps: bfloat16 [10, 41], replicated, may hold values from -1 to 1
Outputs:
- coadd: float32 [64, 512, 512], P('exp', 'grp')
Inputs may be any that keep to these rules, and one draw needn't show every extreme that they name: `tile_exposure`: each exposure is named by exactly 1024 / 512 tiles. `tile_patch`: the entries of a row differ; among the rows of one device no patch is named by more than 2 rows. `tile_offset`: each tile lies wholly inside each patch listed for it.
All inputs are finite; a program needn't handle non-finite values.
Results may differ from a plain program's by a relative error of at most 0.0041.
Values may be sent and summed in bfloat16 or wider, within the bound.
No kernel may reach another device: no remote copies, remote signals or barrier semaphores. Data moves between devices by JAX's collectives and lax.ppermute only.
A program may use at most 128 MiB of HBM per device.

v0:
```python
import math
import jax
import jax.numpy as jnp
from jax import lax
from jax.sharding import PartitionSpec as P

PS = 512


def band_matrix(filters, tile_side):
    terms, kernel_width = filters.shape
    half_width = (kernel_width - 1) // 2
    padding = tile_side - 1 - half_width
    padded = jnp.concatenate(
        [
            jnp.zeros((terms, padding), jnp.float32),
            filters.astype(jnp.float32),
            jnp.zeros((terms, padding + 1), jnp.float32),
        ],
        axis=1,
    )
    tiled = jnp.tile(padded, (1, tile_side + 1))[:, : tile_side * (2 * tile_side + 1)]
    window = tiled.reshape(terms, tile_side, 2 * tile_side + 1)[:, :, :tile_side]
    return window[:, ::-1, :].astype(jnp.bfloat16)


def coverage_rows(tags, row_count, tile_side, patch_side):
    weights = tags[:, 0].astype(jnp.float32)
    row_off = tags[:, 1].astype(jnp.int32)
    col_off = tags[:, 2].astype(jnp.int32)
    row_index = jnp.arange(row_count, dtype=jnp.int32)
    col_index = jnp.arange(patch_side, dtype=jnp.int32)
    row_mask = (
        (row_index[None, :] >= row_off[:, None])
        & (row_index[None, :] < row_off[:, None] + tile_side)
    ).astype(jnp.float32) * weights[:, None]
    col_mask = (
        (col_index[None, :] >= col_off[:, None])
        & (col_index[None, :] < col_off[:, None] + tile_side)
    ).astype(jnp.float32)
    return jnp.einsum("sy,sx->yx", row_mask, col_mask, precision=lax.Precision.HIGHEST)


def per_device(
    tiles, tile_exposure, tile_patch, tile_offset, coeffs, inv_var, vert_taps, horiz_taps
):
    n_owners = lax.axis_size("exp")
    tile_count = tiles.shape[0]
    tile_side = tiles.shape[1]
    listed = tile_patch.shape[1]
    entries = tile_count * listed
    capacity = max(2, (entries + n_owners - 1) // n_owners)
    slot_total = n_owners * capacity
    coef_all, weight_all = (
        lax.all_gather(coeffs, ("exp", "grp"), axis=0, tiled=True),
        lax.all_gather(inv_var, ("exp", "grp"), axis=0, tiled=True),
    )
    exposures = coef_all.shape[0]
    picker = (tile_exposure[:, None] == jnp.arange(exposures, dtype=jnp.int32)[None, :]).astype(
        jnp.bfloat16
    )
    coef_tile = jnp.dot(picker, coef_all, preferred_element_type=jnp.float32)
    weight_tile = jnp.dot(picker, weight_all[:, None], preferred_element_type=jnp.float32)[:, 0]
    vband = band_matrix(vert_taps, tile_side)
    hband = band_matrix(horiz_taps, tile_side)

    def convolve_one(inputs):
        one_tile, coef_row, weight = inputs
        rows_pass = jnp.einsum("yk,bxk->ybx", one_tile, hband, preferred_element_type=jnp.float32)
        partial_value = (rows_pass * coef_row[None, :, None]).astype(jnp.bfloat16)
        smoothed = jnp.einsum(
            "byk,kbx->yx", vband, partial_value, preferred_element_type=jnp.float32
        )
        return (weight * smoothed).astype(jnp.bfloat16)

    weighted = lax.map(convolve_one, (tiles, coef_tile, weight_tile))
    owners = tile_patch.reshape(entries)
    onehot = (owners[:, None] == jnp.arange(n_owners, dtype=jnp.int32)[None, :]).astype(jnp.int32)
    before = jnp.cumsum(onehot, axis=0) - onehot
    rank = jnp.sum(before * onehot, axis=1)
    target = owners * capacity + rank
    offsets = tile_offset.reshape(entries, 2)
    entry_tiles = jnp.repeat(weighted, listed, axis=0)
    entry_tags = jnp.stack(
        [
            jnp.repeat(weight_tile, listed),
            offsets[:, 0].astype(jnp.float32),
            offsets[:, 1].astype(jnp.float32),
        ],
        axis=1,
    ).astype(jnp.bfloat16)
    send_tiles = (
        jnp.zeros((slot_total, tile_side, tile_side), jnp.bfloat16).at[target].set(entry_tiles)
    )
    send_tags = jnp.zeros((slot_total, 3), jnp.bfloat16).at[target].set(entry_tags)
    got_tiles, got_tags = (
        lax.all_to_all(send_tiles, "exp", split_axis=0, concat_axis=0, tiled=True),
        lax.all_to_all(send_tags, "exp", split_axis=0, concat_axis=0, tiled=True),
    )
    got_rows = got_tags[:, 1].astype(jnp.int32)
    got_cols = got_tags[:, 2].astype(jnp.int32)
    block_slots = math.gcd(slot_total, 32)
    block_count = slot_total // block_slots
    inner = jnp.arange(tile_side, dtype=jnp.int32)
    col_index = jnp.arange(PS, dtype=jnp.int32)

    def place_block(canvas, inputs):
        block_tiles, block_rows, block_cols = inputs
        shifter = (
            col_index[None, None, :] == block_cols[:, None, None] + inner[None, :, None]
        ).astype(jnp.bfloat16)
        shifted = jnp.einsum(
            "syk,skx->syx", block_tiles, shifter, preferred_element_type=jnp.float32
        )
        row_index = (block_rows[:, None] + inner[None, :]).reshape(-1)
        canvas = canvas.at[row_index].add(shifted.reshape(-1, PS))
        return (canvas, None)

    flux, _ = lax.scan(
        place_block,
        jnp.zeros((PS, PS), jnp.float32),
        (
            got_tiles.reshape(block_count, block_slots, tile_side, tile_side),
            got_rows.reshape(block_count, block_slots),
            got_cols.reshape(block_count, block_slots),
        ),
    )
    cover = coverage_rows(got_tags, PS, tile_side, PS)
    flux_band, cover_band = (
        lax.psum_scatter(flux, "grp", scatter_dimension=0, tiled=True),
        lax.psum_scatter(cover, "grp", scatter_dimension=0, tiled=True),
    )
    coadd = flux_band / jnp.maximum(cover_band, 1.0)
    return coadd[None]


def solution(mesh):
    in_specs = (
        P(("exp", "grp"), None, None),
        P(("exp", "grp")),
        P(("exp", "grp"), None),
        P(("exp", "grp"), None, None),
        P(("exp", "grp"), None),
        P(("exp", "grp")),
        P(),
        P(),
    )
    out_specs = P("exp", "grp", None)
    return jax.shard_map(
        per_device, mesh=mesh, in_specs=in_specs, out_specs=out_specs, check_vma=False
    )
```

profile of v0, /device:TPU:8, one launch (start us, length us, event | category | flops | bytes accessed | tf_op | source)
XLA Modules:
  0.0 925.7 jit_solution(5432011449631272837)
XLA Ops:
  9.2 78.6 %all-reduce = bf16[512]{0:T(512)(128)(2,1)S(1)} all-reduce(bf16[512]{0:T(512)(128)(2,1)S(1)} %dynamic-update-slice), channel_id=1, replica_groups=mesh['exp'=64,'grp'=4] {'exp','grp'}, use_global_device_ids=true, to_apply=%add | all-reduce | flops 512 | bytes 2048
  90.9 8.2 all-to-all-start
  104.2 8.3 reshape.146
  113.7 19.4 %rev.6 = bf16[10,256,256]{2,1,0:T(8,128)(2,1)} reverse(bf16[10,256,256]{2,1,0:T(8,128)(2,1)} %slice.40), dimensions={1} | reverse | bytes 2621440 | tf_op jit(solution)/shard_map/rev | solution.py:24
  137.2 8.3 reshape.147
  146.7 15.8 %rev.7 = bf16[10,256,256]{2,1,0:T(8,128)(2,1)S(1)} reverse(bf16[10,256,256]{2,1,0:T(8,128)(2,1)} %slice.42), dimensions={1} | reverse | bytes 2621440 | tf_op jit(solution)/shard_map/rev | solution.py:24
  162.5 89.8 %all-gather = bf16[256,2,10]{2,1,0:T(2,128)(2,1)S(1)} all-gather(bf16[1,2,10]{2,1,0:T(2,128)(2,1)S(1)} %bitcast.109), channel_id=1, replica_groups=mesh['exp'=64,'grp'=4] {'exp','grp'}, dimensions={0}, use_global_device_ids=true | all-gather | bytes 10280 | tf_op jit(solution)/shard_map/all_gather | solution.py:55
  252.5 19.2 %while.22 = (s32[]{:T(128)}, bf16[4,256,256]{2,1,0:T(8,128)(2,1)}, f32[4]{0:T(128)S(1)}, bf16[4,256,256]{2,1,0:T(8,128)(2,1)}, bf16[10,256,256]{2,1,0:T(8,128)(2...) while((s32[]{:T(128)}, bf16[4,256,256]{2,1,0:T(8,128)(2,1)}, f32[4]{0:T(128)S(1)}, ...), condition=%wide.region_3.4_spmd, body=%wide.region_2.3_spmd.sunk | while | flops 672530432 | bytes 3409629 | solution.py:76
  258.0 3.3 fusion.66
  267.6 3.3 fusion.66
  273.0 5.9 broadcast_in_dim.28
  278.9 5.3 scatter_fusion.1
  284.2 9.3 %all-to-all-start.1 = ((bf16[128,256,256]{2,1,0:T(8,128)(2,1)}), bf16[128,256,256]{2,1,0:T(8,128)(2,1)}, u32[]{:S(2)}, u32[]{:S(2)}) async-start(bf16[128,256,256]{2,1,0:T(8,128)(2,1)} %scatter_fusion.1), calls=%async_computation.1 | async-start | bytes 33554432 | tf_op jit(solution)/shard_map/all_to_all | solution.py:97
  295.9 363.0 %all-to-all-done.1 = bf16[128,256,256]{2,1,0:T(8,128)(2,1)} async-done(((bf16[128,256,256]{2,1,0:T(8,128)(2,1)}), bf16[128,256,256]{2,1,0:T(8,128)(2,1)}, u32[]{:S(2)}, u32[]{:S(2)}) %all-to-all-start.1) | async-done | bytes 16777248 | tf_op jit(solution)/shard_map/all_to_all | solution.py:97
  659.0 234.6 %while.23 = (s32[]{:T(128)}, f32[512,512]{1,0:T(8,128)S(1)}, s32[4,32]{1,0:T(4,128)S(1)}, bf16[4,32,256,256]{3,2,1,0:T(8,128)(2,1)}, s32[4,32]{1,0:T(4,128)S(1)}, /*index=5*/s32[]{:T(128)}) while((s32[]{:T(128)}, f32[512,512]{1,0:T(8,128)S(1)}, s32[4,32]{1,0:T(4,128)S(1)}, bf16[4,32,256,256]{3,2,1,0:T(8,128)(2,1)}, ...), condition=%wide.region_8.9_spmd.clone.clone, body=%wide.region_6.8_spmd.clone.clone.sunk | while | flops 2155913216 | bytes 71566664 | solution.py:119
  659.3 8.8 fusion.70
  668.3 49.5 %scatter_fusion = f32[512,512]{1,0:T(8,128)S(1)} fusion(f32[512,512]{1,0:T(8,128)S(1)} %get-tuple-element.267, s32[8192]{0:T(1024)S(1)} %bitcast.105, f32[8192,512]{1,0:T(8,128)} %bitcast.99), kind=kCustom, calls=%fused_computation.clone.clone.1 | custom fusion | flops 4194304 | bytes 50364416 | tf_op jit(solution)/shard_map/while/body/eval_jaxpr/scatter-add | solution.py:116
  717.9 8.8 fusion.70
  726.9 49.5 %scatter_fusion = f32[512,512]{1,0:T(8,128)S(1)} fusion(f32[512,512]{1,0:T(8,128)S(1)} %get-tuple-element.267, s32[8192]{0:T(1024)S(1)} %bitcast.105, f32[8192,512]{1,0:T(8,128)} %bitcast.99), kind=kCustom, calls=%fused_computation.clone.clone.1 | custom fusion | flops 4194304 | bytes 50364416 | tf_op jit(solution)/shard_map/while/body/eval_jaxpr/scatter-add | solution.py:116
  776.5 8.8 fusion.70
  785.5 49.5 %scatter_fusion = f32[512,512]{1,0:T(8,128)S(1)} fusion(f32[512,512]{1,0:T(8,128)S(1)} %get-tuple-element.267, s32[8192]{0:T(1024)S(1)} %bitcast.105, f32[8192,512]{1,0:T(8,128)} %bitcast.99), kind=kCustom, calls=%fused_computation.clone.clone.1 | custom fusion | flops 4194304 | bytes 50364416 | tf_op jit(solution)/shard_map/while/body/eval_jaxpr/scatter-add | solution.py:116
  835.0 8.8 fusion.70
  844.0 49.5 %scatter_fusion = f32[512,512]{1,0:T(8,128)S(1)} fusion(f32[512,512]{1,0:T(8,128)S(1)} %get-tuple-element.267, s32[8192]{0:T(1024)S(1)} %bitcast.105, f32[8192,512]{1,0:T(8,128)} %bitcast.99), kind=kCustom, calls=%fused_computation.clone.clone.1 | custom fusion | flops 4194304 | bytes 50364416 | tf_op jit(solution)/shard_map/while/body/eval_jaxpr/scatter-add | solution.py:116
  894.6 22.5 %reduce-scatter.3.cloned.1.call-done = f32[128,512]{1,0:T(8,128)} async-done(((f32[512,512]{1,0:T(8,128)}), f32[128,512]{1,0:T(8,128)}) %reduce-scatter.3.cloned.1.call-update) | async-done | bytes 262160 | tf_op jit(solution)/shard_map/reduce_scatter | solution.py:130
  (99 shorter events, 37.3 us)
Async XLA Ops:
  90.9 193.3 %all-to-all-start = ((bf16[64,2,3]{2,1,0:T(2,128)(2,1)}), bf16[64,2,3]{2,1,0:T(2,128)(2,1)S(1)}, u32[]{:S(2)}, u32[]{:S(2)}) async-start(bf16[64,2,3]{2,1,0:T(2,128)(2,1)} %bitcast.10), calls=%async_computation | async-start | bytes 65536 | tf_op jit(solution)/shard_map/all_to_all | solution.py:98
  145.5 17.0 %copy-start.1 = (bf16[2,10]{1,0:T(2,128)(2,1)S(1)}, bf16[2,10]{1,0:T(2,128)(2,1)}, u32[]{:S(2)}) copy-start(bf16[2,10]{1,0:T(2,128)(2,1)} %param.16) | copy-start | bytes 124
  145.5 106.8 %copy-start.2 = (s32[4]{0:T(128)S(1)}, s32[4]{0:T(128)}, u32[]{:S(2)}) copy-start(s32[4]{0:T(128)} %param.13) | copy-start | bytes 52
  284.2 374.7 %all-to-all-start.1 = ((bf16[128,256,256]{2,1,0:T(8,128)(2,1)}), bf16[128,256,256]{2,1,0:T(8,128)(2,1)}, u32[]{:S(2)}, u32[]{:S(2)}) async-start(bf16[128,256,256]{2,1,0:T(8,128)(2,1)} %scatter_fusion.1), calls=%async_computation.1 | async-start | bytes 33554432 | tf_op jit(solution)/shard_map/all_to_all | solution.py:97
  293.5 601.1 %reduce-scatter.5.cloned.1.call-start = ((), (), s32[]{:S(2)}) async-start(), calls=%async_computation.5 | async-start | bytes 1310720 | tf_op jit(solution)/shard_map/reduce_scatter | solution.py:131
  295.7 621.4 %reduce-scatter.3.cloned.1.call-start = ((), (), s32[]{:S(2)}) async-start(), calls=%async_computation.4 | async-start | bytes 1310720 | tf_op jit(solution)/shard_map/reduce_scatter | solution.py:130
  893.5 1.0 copy-start
Sparse Core Ops, SparseCore 0:
  296.8 26.3 reduce-scatter.4
  894.7 22.3 reduce-scatter.2
where the time goes:
time: 930 us; the launch traced here: 926 us
  waiting for transfers between devices  385 us (41%)
  other arithmetic  202 us (22%)
  blocking collectives  168 us (18%)
  local copies, waits for them, and re-layouts  86.4 us (9%)
  matrix products  51.4 us (6%)
  starting transfers between devices  17.6 us (2%)
  between operations  13.6 us (1%)
    all_to_all x1, waiting for transfers between devices, per_device(): lax.all_to_all(send_tiles, 'exp', split_axis=0, concat_axis=0, tiled=True)  363 us
    scatter-add x4, other arithmetic, place_block(): canvas = canvas.at[row_index].add(shifted.reshape(-1, PS))  198 us
    all_gather x1, blocking collectives, per_device(): lax.all_gather(coeffs, ('exp', 'grp'), axis=0, tiled=True)  89.8 us
    unnamed x1, blocking collectives  78.6 us
    dot_general x4, matrix products, place_block(): jnp.einsum('syk,skx->syx', block_tiles, shifter, preferred_element_type=j...  35.3 us
    rev x2, local copies, waits for them, and re-layouts, band_matrix(): return window[:, ::-1, :].astype(jnp.bfloat16)  35.2 us
    reduce_scatter x1, waiting for transfers between devices, per_device(): lax.psum_scatter(flux, 'grp', scatter_dimension=0, tiled=True)  22.5 us
  transfers between devices with their start and end apart: 4, of which 2 were waited for; matrix products, arithmetic and copies ran while one was open for 36% of the time, Pallas kernels for 0%

commit v1 on v0

--- a/solution.py
+++ b/solution.py
@@ -52,7 +52,12 @@
     capacity = max(2, (entries + n_owners - 1) // n_owners)
     slot_total = n_owners * capacity
     coef_all, weight_all = (
-        lax.all_gather(coeffs, ("exp", "grp"), axis=0, tiled=True),
+        jnp.concatenate(
+            lax.all_to_all(
+                jnp.stack([coeffs] * lax.axis_size(("exp", "grp"))), ("exp", "grp"), 0, 0
+            ),
+            axis=0,
+        ),
         lax.all_gather(inv_var, ("exp", "grp"), axis=0, tiled=True),
     )
     exposures = coef_all.shape[0]

time: 930 us -> 855 us (0.919)
  blocking collectives: 168 us -> 77.4 us
  starting transfers between devices: 17.6 us -> 33.9 us
    all_gather x1 -> x0, blocking collectives: 89.8 us -> none  [per_device(): lax.all_gather(coeffs, ('exp', 'grp'), axis=0, tiled=True)]
    all_to_all x0 -> x1, starting transfers between devices: none -> 14.6 us  [per_device(): lax.all_to_all(jnp.stack([coeffs] * lax.axis_size(('exp', 'grp'))), ('exp...]
  transfers between devices with their start and end apart: 4 -> 5, of which waited for: 2 -> 2; matrix products, arithmetic and copies ran while one was open for 36% -> 40% of each run, Pallas kernels for 0% -> 0%
where the time goes in v1:
time: 855 us; the launch traced here: 851 us
  waiting for transfers between devices  384 us (45%)
  other arithmetic  202 us (24%)
  local copies, waits for them, and re-layouts  87.4 us (10%)
  blocking collectives  77.4 us (9%)
  matrix products  51.3 us (6%)
  starting transfers between devices  33.9 us (4%)
  between operations  13.6 us (2%)
    all_to_all x1, waiting for transfers between devices, per_device(): lax.all_to_all(send_tiles, 'exp', split_axis=0, concat_axis=0, tiled=True)  363 us
    scatter-add x4, other arithmetic, place_block(): canvas = canvas.at[row_index].add(shifted.reshape(-1, PS))  198 us
    unnamed x1, blocking collectives  77.4 us
    dot_general x4, matrix products, place_block(): jnp.einsum('syk,skx->syx', block_tiles, shifter, preferred_element_type=j...  35.3 us
    rev x2, local copies, waits for them, and re-layouts, band_matrix(): return window[:, ::-1, :].astype(jnp.bfloat16)  35.2 us
    reduce_scatter x1, waiting for transfers between devices, per_device(): lax.psum_scatter(flux, 'grp', scatter_dimension=0, tiled=True)  21.4 us
  transfers between devices with their start and end apart: 5, of which 2 were waited for; matrix products, arithmetic and copies ran while one was open for 40% of the time, Pallas kernels for 0%

profile of v1, /device:TPU:8, one launch (start us, length us, event | category | flops | bytes accessed | tf_op | source)
XLA Modules:
  0.0 850.7 jit_solution(4699662942953374087)
XLA Ops:
  7.9 14.6 %all-to-all-start.1 = ((bf16[256,2,10]{2,1,0:T(2,128)(2,1)}), bf16[256,2,10]{2,1,0:T(2,128)(2,1)S(1)}, u32[]{:S(2)}, u32[]{:S(2)}) async-start(bf16[256,2,10]{2,1,0:T(2,128)(2,1)} %stack.6), calls=%async_computation.1 | async-start | bytes 262144 | tf_op jit(solution)/shard_map/all_to_all | solution.py:56
  25.2 77.4 %all-reduce = bf16[512]{0:T(512)(128)(2,1)S(1)} all-reduce(bf16[512]{0:T(512)(128)(2,1)S(1)} %dynamic-update-slice), channel_id=1, replica_groups=mesh['exp'=64,'grp'=4] {'exp','grp'}, use_global_device_ids=true, to_apply=%add | all-reduce | flops 512 | bytes 2048
  109.5 8.3 reshape.151
  119.0 19.4 %rev.6 = bf16[10,256,256]{2,1,0:T(8,128)(2,1)} reverse(bf16[10,256,256]{2,1,0:T(8,128)(2,1)} %slice.40), dimensions={1} | reverse | bytes 2621440 | tf_op jit(solution)/shard_map/rev | solution.py:24
  142.5 8.3 reshape.153
  152.1 15.8 %rev.7 = bf16[10,256,256]{2,1,0:T(8,128)(2,1)S(1)} reverse(bf16[10,256,256]{2,1,0:T(8,128)(2,1)} %slice.42), dimensions={1} | reverse | bytes 2621440 | tf_op jit(solution)/shard_map/rev | solution.py:24
  169.1 8.8 %all-to-all-start = ((bf16[64,2,3]{2,1,0:T(2,128)(2,1)}), bf16[64,2,3]{2,1,0:T(2,128)(2,1)S(1)}, u32[]{:S(2)}, u32[]{:S(2)}) async-start(bf16[64,2,3]{2,1,0:T(2,128)(2,1)} %bitcast.10), calls=%async_computation | async-start | bytes 65536 | tf_op jit(solution)/shard_map/all_to_all | solution.py:103
  178.0 18.7 %while.22 = (s32[]{:T(128)}, bf16[4,256,256]{2,1,0:T(8,128)(2,1)}, f32[4]{0:T(128)S(1)}, bf16[4,256,256]{2,1,0:T(8,128)(2,1)}, bf16[10,256,256]{2,1,0:T(8,128)(2...) while((s32[]{:T(128)}, bf16[4,256,256]{2,1,0:T(8,128)(2,1)}, f32[4]{0:T(128)S(1)}, ...), condition=%wide.region_3.4_spmd, body=%wide.region_2.3_spmd.sunk | while | flops 672530432 | bytes 3409629 | solution.py:81
  178.6 3.3 fusion.66
  183.3 3.3 fusion.66
  198.0 5.9 broadcast_in_dim.28
  204.0 5.3 scatter_fusion.1
  209.2 10.4 %all-to-all-start.2 = ((bf16[128,256,256]{2,1,0:T(8,128)(2,1)}), bf16[128,256,256]{2,1,0:T(8,128)(2,1)}, u32[]{:S(2)}, u32[]{:S(2)}) async-start(bf16[128,256,256]{2,1,0:T(8,128)(2,1)} %scatter_fusion.1), calls=%async_computation.2 | async-start | bytes 33554432 | tf_op jit(solution)/shard_map/all_to_all | solution.py:102
  222.1 363.0 %all-to-all-done.2 = bf16[128,256,256]{2,1,0:T(8,128)(2,1)} async-done(((bf16[128,256,256]{2,1,0:T(8,128)(2,1)}), bf16[128,256,256]{2,1,0:T(8,128)(2,1)}, u32[]{:S(2)}, u32[]{:S(2)}) %all-to-all-start.2) | async-done | bytes 16777248 | tf_op jit(solution)/shard_map/all_to_all | solution.py:102
  585.2 234.5 %while.23 = (s32[]{:T(128)}, f32[512,512]{1,0:T(8,128)S(1)}, s32[4,32]{1,0:T(4,128)S(1)}, bf16[4,32,256,256]{3,2,1,0:T(8,128)(2,1)}, s32[4,32]{1,0:T(4,128)S(1)}, /*index=5*/s32[]{:T(128)}) while((s32[]{:T(128)}, f32[512,512]{1,0:T(8,128)S(1)}, s32[4,32]{1,0:T(4,128)S(1)}, bf16[4,32,256,256]{3,2,1,0:T(8,128)(2,1)}, ...), condition=%wide.region_8.9_spmd.clone.clone, body=%wide.region_6.8_spmd.clone.clone.sunk | while | flops 2155913216 | bytes 71566664 | solution.py:124
  585.5 8.8 %fusion.70 = f32[32,256,512]{2,1,0:T(8,128)} fusion(s32[32,256]{1,0:T(8,128)S(1)} %iota_add_fusion.3, bf16[4,32,256,256]{3,2,1,0:T(8,128)(2,1)} %get-tuple-element.275, s32[]{:T(128)} %get-tuple-element.266), kind=kOutput, calls=%fused_computation.19.clone.1 | convolution fusion | flops 2151677952 | bytes 21004800 | tf_op jit(solution)/shard_map/while/body/eval_jaxpr/syk,skx->syx/dot_general | solution.py:117
  594.5 49.5 %scatter_fusion = f32[512,512]{1,0:T(8,128)S(1)} fusion(f32[512,512]{1,0:T(8,128)S(1)} %get-tuple-element.267, s32[8192]{0:T(1024)S(1)} %bitcast.104, f32[8192,512]{1,0:T(8,128)} %bitcast.98), kind=kCustom, calls=%fused_computation.clone.clone.1 | custom fusion | flops 4194304 | bytes 50364416 | tf_op jit(solution)/shard_map/while/body/eval_jaxpr/scatter-add | solution.py:121
  644.1 8.8 %fusion.70 = f32[32,256,512]{2,1,0:T(8,128)} fusion(s32[32,256]{1,0:T(8,128)S(1)} %iota_add_fusion.3, bf16[4,32,256,256]{3,2,1,0:T(8,128)(2,1)} %get-tuple-element.275, s32[]{:T(128)} %get-tuple-element.266), kind=kOutput, calls=%fused_computation.19.clone.1 | convolution fusion | flops 2151677952 | bytes 21004800 | tf_op jit(solution)/shard_map/while/body/eval_jaxpr/syk,skx->syx/dot_general | solution.py:117
  653.0 49.5 %scatter_fusion = f32[512,512]{1,0:T(8,128)S(1)} fusion(f32[512,512]{1,0:T(8,128)S(1)} %get-tuple-element.267, s32[8192]{0:T(1024)S(1)} %bitcast.104, f32[8192,512]{1,0:T(8,128)} %bitcast.98), kind=kCustom, calls=%fused_computation.clone.clone.1 | custom fusion | flops 4194304 | bytes 50364416 | tf_op jit(solution)/shard_map/while/body/eval_jaxpr/scatter-add | solution.py:121
  702.6 8.8 %fusion.70 = f32[32,256,512]{2,1,0:T(8,128)} fusion(s32[32,256]{1,0:T(8,128)S(1)} %iota_add_fusion.3, bf16[4,32,256,256]{3,2,1,0:T(8,128)(2,1)} %get-tuple-element.275, s32[]{:T(128)} %get-tuple-element.266), kind=kOutput, calls=%fused_computation.19.clone.1 | convolution fusion | flops 2151677952 | bytes 21004800 | tf_op jit(solution)/shard_map/while/body/eval_jaxpr/syk,skx->syx/dot_general | solution.py:117
  711.6 49.5 %scatter_fusion = f32[512,512]{1,0:T(8,128)S(1)} fusion(f32[512,512]{1,0:T(8,128)S(1)} %get-tuple-element.267, s32[8192]{0:T(1024)S(1)} %bitcast.104, f32[8192,512]{1,0:T(8,128)} %bitcast.98), kind=kCustom, calls=%fused_computation.clone.clone.1 | custom fusion | flops 4194304 | bytes 50364416 | tf_op jit(solution)/shard_map/while/body/eval_jaxpr/scatter-add | solution.py:121
  761.2 8.8 %fusion.70 = f32[32,256,512]{2,1,0:T(8,128)} fusion(s32[32,256]{1,0:T(8,128)S(1)} %iota_add_fusion.3, bf16[4,32,256,256]{3,2,1,0:T(8,128)(2,1)} %get-tuple-element.275, s32[]{:T(128)} %get-tuple-element.266), kind=kOutput, calls=%fused_computation.19.clone.1 | convolution fusion | flops 2151677952 | bytes 21004800 | tf_op jit(solution)/shard_map/while/body/eval_jaxpr/syk,skx->syx/dot_general | solution.py:117
  770.2 49.5 %scatter_fusion = f32[512,512]{1,0:T(8,128)S(1)} fusion(f32[512,512]{1,0:T(8,128)S(1)} %get-tuple-element.267, s32[8192]{0:T(1024)S(1)} %bitcast.104, f32[8192,512]{1,0:T(8,128)} %bitcast.98), kind=kCustom, calls=%fused_computation.clone.clone.1 | custom fusion | flops 4194304 | bytes 50364416 | tf_op jit(solution)/shard_map/while/body/eval_jaxpr/scatter-add | solution.py:121
  820.7 21.4 %reduce-scatter.3.cloned.1.call-done = f32[128,512]{1,0:T(8,128)} async-done(((f32[512,512]{1,0:T(8,128)}), f32[128,512]{1,0:T(8,128)}) %reduce-scatter.3.cloned.1.call-update) | async-done | bytes 262160 | tf_op jit(solution)/shard_map/reduce_scatter | solution.py:135
  (99 shorter events, 38.3 us)
Async XLA Ops:
  7.9 161.1 %all-to-all-start.1 = ((bf16[256,2,10]{2,1,0:T(2,128)(2,1)}), bf16[256,2,10]{2,1,0:T(2,128)(2,1)S(1)}, u32[]{:S(2)}, u32[]{:S(2)}) async-start(bf16[256,2,10]{2,1,0:T(2,128)(2,1)} %stack.6), calls=%async_computation.1 | async-start | bytes 262144 | tf_op jit(solution)/shard_map/all_to_all | solution.py:56
  150.9 27.0 %copy-start.1 = (s32[4]{0:T(128)S(1)}, s32[4]{0:T(128)}, u32[]{:S(2)}) copy-start(s32[4]{0:T(128)} %param.13) | copy-start | bytes 52
  169.1 40.2 %all-to-all-start = ((bf16[64,2,3]{2,1,0:T(2,128)(2,1)}), bf16[64,2,3]{2,1,0:T(2,128)(2,1)S(1)}, u32[]{:S(2)}, u32[]{:S(2)}) async-start(bf16[64,2,3]{2,1,0:T(2,128)(2,1)} %bitcast.10), calls=%async_computation | async-start | bytes 65536 | tf_op jit(solution)/shard_map/all_to_all | solution.py:103
  209.2 375.8 %all-to-all-start.2 = ((bf16[128,256,256]{2,1,0:T(8,128)(2,1)}), bf16[128,256,256]{2,1,0:T(8,128)(2,1)}, u32[]{:S(2)}, u32[]{:S(2)}) async-start(bf16[128,256,256]{2,1,0:T(8,128)(2,1)} %scatter_fusion.1), calls=%async_computation.2 | async-start | bytes 33554432 | tf_op jit(solution)/shard_map/all_to_all | solution.py:102
  219.7 601.1 %reduce-scatter.5.cloned.1.call-start = ((), (), s32[]{:S(2)}) async-start(), calls=%async_computation.6 | async-start | bytes 1310720 | tf_op jit(solution)/shard_map/reduce_scatter | solution.py:136
  221.9 620.2 %reduce-scatter.3.cloned.1.call-start = ((), (), s32[]{:S(2)}) async-start(), calls=%async_computation.5 | async-start | bytes 1310720 | tf_op jit(solution)/shard_map/reduce_scatter | solution.py:135
  819.7 1.0 copy-start
Sparse Core Ops, SparseCore 0:
  223.0 25.2 reduce-scatter.4
  820.8 21.2 reduce-scatter.2
